TPU v7x, 256 devices: a whole 4x4x8 slice. The times are simulated.
256 devices in a mesh: tok: 16 (over z, core), tp: 16 (over x, y).
Axes of the slice: x: 4, y: 4, z: 8, core: 2. Of those that a mesh axis runs over, the one named last changes fastest.
Arguments:
- hidden_states: bfloat16 [32768, 1024], P(('tok', 'tp')), may hold values from -40 to 40
- first_gain: float32 [1024], replicated, may hold values from 0.1 to 1.9
- second_gain: float32 [1024], replicated, may hold values from 0.1 to 1.9
- w_query: bfloat16 [1024, 1024], P(None, 'tp'), may hold values from -1 to 1
- w_keyval: bfloat16 [1024, 1024], replicated, may hold values from -0.375 to 0.375
- w_out: bfloat16 [1024, 1024], P('tp'), may hold values from -0.75 to 0.75
- kv_cache: bfloat16 [384, 128, 1024], P('tok'), may hold values from -310 to 310
- page_table: int32 [32, 16], P('tok'), may hold values from 0 to 383, as said below
- cached_len: int32 [32], P('tok'), may hold values from 128 to 2048, as said below
- expert_ids: int32 [32768, 8], P(('tok', 'tp')), may hold values from 0 to 31, all different within a row; in each aligned block of 128 rows (0 to 127, 128 to 255, ...) at most 64 rows name the same one
- gate_weights: float32 [32768, 8], P(('tok', 'tp')), may hold values from 0.1 to 1
- w_gate_up: bfloat16 [32, 1024, 1024], P('tp', 'tok'), may hold values from -0.1875 to 0.1875
- w_down: bfloat16 [32, 512, 1024], P('tp', 'tok'), may hold values from -1 to 1
Outputs:
- layer_out: bfloat16 [32768, 1024], P(('tok', 'tp'))
Inputs may be any that keep to these rules, and one draw needn't show every extreme that they name: `page_table`: request r's entries are pages of its own tok index, rows 24 * (r // 2) to 24 * (r // 2 + 1) - 1; its first 8 entries are the same for all requests of that tok index, and all other entries name pages that no other entry names. `cached_len`: some request has exactly 2048 cached tokens. `expert_ids`: in the rows of one device (aligned blocks of 128 rows) no expert is named by more than 64 rows, and a row names 8 different experts.
All inputs are finite; a program needn't handle non-finite values.
Results may differ from a plain program's by a relative error of at most 0.017.
The roundings to bfloat16 on the way count: a program that leaves them out, or rounds other values in their place, can miss the bound.
Values may be sent and summed in bfloat16 or wider, within the bound.
No kernel may reach another device: no remote copies, remote signals or barrier semaphores. Data moves between devices by JAX's collectives and lax.ppermute only.
A program may use at most 128 MiB of HBM per device.

v0:
```python
import jax
import jax.numpy as jnp
from jax import lax
from jax.sharding import PartitionSpec as P

D = 1024
HEADS = 16
KV_HEADS = 8
HEAD_DIM = 64
EXPERTS = 32
FF_EXPERT = 512
TOP = 8
NEW = 1024
MAX_CACHED = 2048
REQ_DEV = 2


ATTN_SCALE = 0.015625
EPSILON = 1e-06
THETA = 10000.0


def rms_norm(values, gain):
    wide = values.astype(jnp.float32)
    factor = lax.rsqrt(jnp.mean(wide * wide, axis=-1, keepdims=True) + EPSILON)
    return (wide * factor * gain).astype(jnp.bfloat16)


def rotate(values, positions):
    row_count = values.shape[0]
    shaped = values.reshape(row_count, -1, HEAD_DIM)
    half_dim = HEAD_DIM // 2
    exponent = jnp.arange(half_dim).astype(jnp.float32) * (2.0 / HEAD_DIM)
    frequency = jnp.power(THETA, -exponent)
    angles = positions.astype(jnp.float32)[:, None] * frequency[None, :]
    cosine = jnp.cos(angles)[:, None, :]
    sine_part = jnp.sin(angles)[:, None, :]
    leading = shaped[..., :half_dim]
    trailing = shaped[..., half_dim:]
    turned = jnp.concatenate(
        [leading * cosine - trailing * sine_part, trailing * cosine + leading * sine_part], axis=-1
    )
    return turned.reshape(row_count, -1)


def attend_request(queries, keys_total, values_total, length):
    block_rows = min(NEW, 512)
    key_index = jnp.arange(MAX_CACHED + NEW, dtype=jnp.int32)

    def one_block(block_start):
        block_query = lax.dynamic_slice_in_dim(queries, block_start, block_rows, 0)
        scores = (
            jnp.einsum(
                "qgpd,kgd->gpqk", block_query, keys_total, preferred_element_type=jnp.float32
            )
            * ATTN_SCALE
        )
        query_pos = block_start + jnp.arange(block_rows, dtype=jnp.int32)
        allowed = jnp.where(
            key_index[None, :] < MAX_CACHED,
            key_index[None, :] < length,
            key_index[None, :] - MAX_CACHED <= query_pos[:, None],
        )
        scores = jnp.where(allowed, scores, -1e30)
        top_score = jnp.max(scores, axis=-1, keepdims=True)
        weights = jnp.exp(scores - top_score)
        probs = (weights / jnp.sum(weights, axis=-1, keepdims=True)).astype(jnp.bfloat16)
        mixed = jnp.einsum(
            "gpqk,kgd->qgpd", probs, values_total, preferred_element_type=jnp.float32
        )
        return mixed.astype(jnp.bfloat16).reshape(block_rows, -1)

    starts = jnp.arange(NEW // block_rows, dtype=jnp.int32) * block_rows
    return lax.map(one_block, starts).reshape(NEW, -1)


def shards(
    hidden_states,
    first_gain,
    second_gain,
    w_query,
    w_keyval,
    w_out,
    kv_cache,
    page_table,
    cached_len,
    expert_ids,
    gate_weights,
    w_gate_up,
    w_down,
):
    gate_up_full, down_full = (
        lax.all_gather(w_gate_up, "tok", axis=1, tiled=True),
        lax.all_gather(w_down, "tok", axis=1, tiled=True),
    )
    tok_rows = hidden_states.shape[0]
    tp_size = lax.axis_size("tp")
    tp_rank = lax.axis_index("tp")
    local_heads = HEADS // tp_size
    group_size = HEADS // KV_HEADS
    local_kv = max(local_heads // group_size, 1)
    per_group = local_heads // local_kv
    head_width = local_heads * HEAD_DIM
    kv_width = local_kv * HEAD_DIM
    kv_cols = KV_HEADS * HEAD_DIM
    group_tokens = REQ_DEV * NEW
    first_kv = tp_rank * local_heads // group_size
    request_range = jnp.arange(REQ_DEV, dtype=jnp.int32)
    normed = rms_norm(hidden_states, first_gain)
    key_part = lax.dynamic_slice_in_dim(w_keyval, first_kv * HEAD_DIM, kv_width, 1)
    value_part = lax.dynamic_slice_in_dim(w_keyval, kv_cols + first_kv * HEAD_DIM, kv_width, 1)
    piece = lax.all_gather(normed, "tp", axis=0, tiled=True)
    row_index = jnp.arange(piece.shape[0], dtype=jnp.int32)
    owner = row_index // NEW
    base_len = jnp.sum(
        jnp.where(owner[:, None] == request_range[None, :], cached_len[None, :], 0), axis=1
    )
    piece_pos = base_len + row_index % NEW
    query_rows = rotate(jnp.dot(piece, w_query, preferred_element_type=jnp.float32), piece_pos)
    key_rows = rotate(jnp.dot(piece, key_part, preferred_element_type=jnp.float32), piece_pos)
    value_rows = jnp.dot(piece, value_part, preferred_element_type=jnp.float32)
    projected = jnp.concatenate([query_rows, key_rows, value_rows], axis=1).astype(jnp.bfloat16)
    queries = projected[:, :head_width].reshape(REQ_DEV, NEW, local_kv, per_group, HEAD_DIM)
    new_keys = projected[:, head_width : head_width + kv_width].reshape(
        REQ_DEV, NEW, local_kv, HEAD_DIM
    )
    new_values = projected[:, head_width + kv_width :].reshape(REQ_DEV, NEW, local_kv, HEAD_DIM)
    cache_keys = lax.dynamic_slice_in_dim(kv_cache, first_kv * HEAD_DIM, kv_width, 2)
    cache_values = lax.dynamic_slice_in_dim(kv_cache, kv_cols + first_kv * HEAD_DIM, kv_width, 2)
    local_pages = page_table - lax.axis_index("tok") * kv_cache.shape[0]

    def per_request(inputs):
        page_ids, length, request_q, request_k, request_v = inputs
        keys_total = jnp.concatenate(
            [
                jnp.take(cache_keys, page_ids, axis=0).reshape(MAX_CACHED, local_kv, HEAD_DIM),
                request_k,
            ],
            axis=0,
        )
        values_total = jnp.concatenate(
            [
                jnp.take(cache_values, page_ids, axis=0).reshape(MAX_CACHED, local_kv, HEAD_DIM),
                request_v,
            ],
            axis=0,
        )
        return attend_request(request_q, keys_total, values_total, length)

    attended = lax.map(
        per_request, (local_pages, cached_len, queries, new_keys, new_values)
    ).reshape(group_tokens, head_width)
    projected_out = lax.psum_scatter(
        jnp.dot(attended, w_out, preferred_element_type=jnp.float32),
        "tp",
        scatter_dimension=0,
        tiled=True,
    )
    middle = (hidden_states.astype(jnp.float32) + projected_out).astype(jnp.bfloat16)
    normed_two = rms_norm(middle, second_gain)
    experts_local = EXPERTS // tp_size
    capacity = 2 * tok_rows * TOP // EXPERTS
    expert_range = jnp.arange(EXPERTS, dtype=jnp.int32)
    onehot = (expert_ids[:, :, None] == expert_range[None, None, :]).astype(jnp.int32)
    per_token = jnp.sum(onehot, axis=1)
    earlier = jnp.cumsum(per_token, axis=0) - per_token
    slot_ids = jnp.sum(onehot * earlier[:, None, :], axis=2)
    target = expert_ids * capacity + slot_ids
    outgoing_rows = jnp.broadcast_to(normed_two[:, None, :], (tok_rows, TOP, D))
    send_buffer = jnp.zeros((EXPERTS * capacity, D), jnp.bfloat16).at[target].set(outgoing_rows)
    received = lax.all_to_all(
        send_buffer.reshape(tp_size, experts_local, capacity, D),
        "tp",
        split_axis=0,
        concat_axis=2,
        tiled=True,
    )
    received = received.reshape(experts_local, tp_size * capacity, D)
    both = jnp.einsum("esd,edf->esf", received, gate_up_full, preferred_element_type=jnp.float32)
    activated = (jax.nn.silu(both[..., :FF_EXPERT]) * both[..., FF_EXPERT:]).astype(jnp.bfloat16)
    produced = jnp.einsum(
        "esf,efd->esd", activated, down_full, preferred_element_type=jnp.float32
    ).astype(jnp.bfloat16)
    returned = lax.all_to_all(
        produced.reshape(experts_local, tp_size, capacity, D),
        "tp",
        split_axis=1,
        concat_axis=0,
        tiled=True,
    )
    returned = returned.reshape(EXPERTS * capacity, D)
    picked = returned[target]
    mixture = jnp.einsum("tk,tkd->td", gate_weights, picked.astype(jnp.float32))
    return (middle.astype(jnp.float32) + mixture).astype(jnp.bfloat16)


def solution(mesh):
    in_specs = (
        P(("tok", "tp"), None),
        P(),
        P(),
        P(None, "tp"),
        P(),
        P("tp", None),
        P("tok", None, None),
        P("tok", None),
        P("tok"),
        P(("tok", "tp"), None),
        P(("tok", "tp"), None),
        P("tp", "tok", None),
        P("tp", "tok", None),
    )
    out_specs = P(("tok", "tp"), None)
    return jax.shard_map(shards, mesh=mesh, in_specs=in_specs, out_specs=out_specs, check_vma=False)
```

profile of v0, /device:TPU:224, one launch (start us, length us, event | category | flops | bytes accessed | tf_op | source)
XLA Modules:
  0.0 387.9 jit_solution(955928082948849221)
XLA Ops:
  7.4 1.2 fusion.29
  8.6 1.8 fusion.31
  10.6 0.7 fusion.55
  11.3 2.8 constant_dynamic-slice_fusion.1
  14.1 53.4 %all-gather.4.cloned.1.call-done = bf16[2048,1024]{1,0:T(8,128)(2,1)} async-done(((bf16[128,1024]{1,0:T(8,128)(2,1)}), bf16[2048,1024]{1,0:T(8,128)(2,1)}) %all-gather.4.cloned.1.call-update) | async-done | bytes 4194320 | tf_op jit(solution)/shard_map/all_gather | solution.py:112
  67.5 3.8 convolution_bitcast_fusion
  71.3 1.4 convolution_bitcast_fusion.1
  72.7 1.2 fusion.50
  73.9 0.8 pad_maximum_fusion.2
  74.7 1.1 reshape.360
  75.8 0.8 copy.43
  76.6 3.7 convolution_convert_fusion.1
  80.5 44.6 %while.34 = (s32[]{:T(128)}, bf16[2,1024,64]{2,1,0:T(8,128)(2,1)}, bf16[2,1024,1,1,64]{1,4,3,2,0:T(8,128)(2,1)}, s32[2,16]{1,0:T(2,128)S(1)}, bf16[24,128,64]{2,...) while((s32[]{:T(128)}, bf16[2,1024,64]{2,1,0:T(8,128)(2,1)}, ...), condition=%wide.region_7.9_spmd, body=%wide.region_2.8_spmd.sunk | while | flops 420259424 | bytes 28236604 | solution.py:150
  81.2 1.8 gather_fusion.1
  83.7 0.9 dynamic-slice_bitcast_fusion.5
  85.3 16.5 %while.35 = (s32[]{:T(128)}, bf16[2,512,64]{1,2,0:T(8,128)(2,1)S(1)}, s32[]{:T(128)}, s32[2]{0:T(128)S(1)}, bf16[1024,1,1,64]{0,3,2,1:T(8,128)(2,1)S(1)}, /*inde...) while((s32[]{:T(128)}, ...), condition=%wide.region_6.7_spmd.clone.clone, body=%wide.region_3.6_spmd.clone.clone.sunk | while | flops 418423296 | bytes 19843236 | solution.py:74
  89.1 2.0 fusion.89
  91.1 1.0 fusion.90
  92.1 1.4 fusion.91
  97.3 2.0 fusion.89
  99.3 1.0 fusion.90
  100.3 1.4 fusion.91
  102.0 0.8 copy-done.5
  103.5 1.8 gather_fusion.1
  106.0 0.9 dynamic-slice_bitcast_fusion.5
  107.5 16.5 %while.35 = (s32[]{:T(128)}, bf16[2,512,64]{1,2,0:T(8,128)(2,1)S(1)}, s32[]{:T(128)}, s32[2]{0:T(128)S(1)}, bf16[1024,1,1,64]{0,3,2,1:T(8,128)(2,1)S(1)}, /*inde...) while((s32[]{:T(128)}, ...), condition=%wide.region_6.7_spmd.clone.clone, body=%wide.region_3.6_spmd.clone.clone.sunk | while | flops 418423296 | bytes 19843236 | solution.py:74
  111.3 2.0 fusion.89
  113.3 1.0 fusion.90
  114.3 1.4 fusion.91
  119.6 2.0 fusion.89
  121.6 1.0 fusion.90
  122.6 1.4 fusion.91
  124.3 0.8 copy-done.5
  125.1 5.5 %fusion.70 = f32[2048,1024]{1,0:T(8,128)} fusion(bf16[2048,64]{1,0:T(8,128)(2,1)} %bitcast.130, bf16[64,1024]{1,0:T(8,128)(2,1)S(1)} %copy-done.6), kind=kOutput, calls=%fused_computation.117 | convolution fusion | flops 268435456 | bytes 8781824 | tf_op jit(solution)/shard_map/dot_general | solution.py:154
  131.9 89.4 %reduce-scatter.2.cloned.1.call-done = f32[128,1024]{1,0:T(8,128)} async-done(((f32[2048,1024]{1,0:T(8,128)}), f32[128,1024]{1,0:T(8,128)}) %reduce-scatter.2.cloned.1.call-update) | async-done | bytes 524304 | tf_op jit(solution)/shard_map/reduce_scatter | solution.py:153
  221.2 1.2 fusion.33
  222.6 7.9 %scatter_custom_fusion = bf16[2048,1024]{1,0:T(8,128)(2,1)} fusion(s32[1024]{0:T(1024)S(1)} %reshape.399, bf16[]{:T(256)} %constant.161.clone.1, bf16[128,1024]{1,0:T(8,128)(2,1)S(1)} %fusion.35), kind=kCustom, calls=%fused_computation.45 | custom fusion | bytes 4456450 | tf_op jit(solution)/shard_map/scatter | solution.py:170
  230.5 5.0 %all-to-all-start = ((bf16[16,2,64,1024]{3,2,1,0:T(8,128)(2,1)}), bf16[16,2,64,1024]{3,2,1,0:T(8,128)(2,1)}, u32[]{:S(2)}, u32[]{:S(2)}) async-start(bf16[16,2,64,1024]{3,2,1,0:T(8,128)(2,1)} %bitcast.126), calls=%async_computation.1 | async-start | bytes 8388608 | tf_op jit(solution)/shard_map/all_to_all | solution.py:171
  236.1 53.7 %all-to-all-done = bf16[16,2,64,1024]{3,2,1,0:T(8,128)(2,1)} async-done(((bf16[16,2,64,1024]{3,2,1,0:T(8,128)(2,1)}), bf16[16,2,64,1024]{3,2,1,0:T(8,128)(2,1)}, u32[]{:S(2)}, u32[]{:S(2)}) %all-to-all-start) | async-done | bytes 4194336 | tf_op jit(solution)/shard_map/all_to_all | solution.py:171
  289.8 4.8 %copy.50 = bf16[1,2,16,64,1024]{4,3,2,1,0:T(8,128)(2,1)} copy(bf16[1,2,16,64,1024]{4,3,1,2,0:T(8,128)(2,1)} %bitcast.14) | data formatting | bytes 8388608 | tf_op jit(solution)/shard_map/all_to_all | solution.py:171
  294.6 11.2 %fusion.71 = f32[2,1024,1024]{2,1,0:T(8,128)} fusion(bf16[2,1024,1024]{2,1,0:T(8,128)(2,1)} %bitcast.127, bf16[2,1024,1024]{2,1,0:T(8,128)(2,1)} %all-gather.6.cloned.1.call-done), kind=kOutput, calls=%fused_computation.118 | convolution fusion | flops 4294967296 | bytes 16777216 | tf_op jit(solution)/shard_map/esd,edf->esf/dot_general | solution.py:179
  305.8 6.4 %convolution_convert_fusion = bf16[2,1024,1024]{2,1,0:T(8,128)(2,1)S(1)} fusion(bf16[2,512,1024]{2,1,0:T(8,128)(2,1)} %all-gather.8.cloned.1.call-done, f32[2,1024,1024]{2,1,0:T(8,128)} %fusion.71), kind=kOutput, calls=%fused_computation.39 | convolution fusion | flops 2155872256 | bytes 14680064 | tf_op jit(solution)/shard_map/esf,efd->esd/dot_general | solution.py:181
  312.2 2.4 copy.51
  314.7 4.7 %all-to-all-start.1 = ((bf16[2,16,64,1024]{3,2,0,1:T(8,128)(2,1)}), bf16[2,16,64,1024]{3,2,0,1:T(8,128)(2,1)}, u32[]{:S(2)}, u32[]{:S(2)}) async-start(bf16[2,16,64,1024]{3,2,0,1:T(8,128)(2,1)} %copy.51), calls=%async_computation.2 | async-start | bytes 8388608 | tf_op jit(solution)/shard_map/all_to_all | solution.py:184
  319.5 48.9 %all-to-all-done.1 = bf16[2,16,64,1024]{3,2,0,1:T(8,128)(2,1)} async-done(((bf16[2,16,64,1024]{3,2,0,1:T(8,128)(2,1)}), bf16[2,16,64,1024]{3,2,0,1:T(8,128)(2,1)}, u32[]{:S(2)}, u32[]{:S(2)}) %all-to-all-start.1) | async-done | bytes 4194336 | tf_op jit(solution)/shard_map/all_to_all | solution.py:184
  368.5 8.9 %gather_fusion.2 = bf16[1024,1024]{1,0:T(8,128)(2,1)} fusion(bf16[2048,1024]{1,0:T(8,128)(2,1)} %bitcast.19, s32[1024]{0:T(1024)S(1)} %broadcast_clamp_fusion), kind=kCustom, calls=%fused_computation.2 | custom fusion | bytes 4198400 | tf_op jit(solution)/shard_map/gather | solution.py:192
  377.4 2.3 fusion.22
  379.6 0.8 fusion.36
  (104 shorter events, 14.4 us)
Async XLA Ops:
  7.4 60.1 %copy-start = (bf16[1024,1024]{1,0:T(8,128)(2,1)S(1)}, bf16[1024,1024]{1,0:T(8,128)(2,1)}, u32[]{:S(2)}) copy-start(bf16[1024,1024]{1,0:T(8,128)(2,1)} %param.23) | copy-start | bytes 6291460
  7.4 6.7 %copy-start.11 = (s32[2,16]{1,0:T(2,128)S(1)}, s32[2,16]{1,0:T(2,128)}, u32[]{:S(2)}) copy-start(s32[2,16]{1,0:T(2,128)} %param.26) | copy-start | bytes 388
  7.4 60.1 %all-gather.4.cloned.1.call-start = ((), (), s32[]{:S(2)}) async-start(), calls=%async_computation.3 | async-start | bytes 4456448 | tf_op jit(solution)/shard_map/all_gather | solution.py:112
  10.4 210.8 %reduce-scatter.2.cloned.1.call-start = ((), (), s32[]{:S(2)}) async-start(), calls=%async_computation.4 | async-start | bytes 8912896 | tf_op jit(solution)/shard_map/reduce_scatter | solution.py:153
  14.1 57.2 %copy-start.7 = (bf16[1024,64]{0,1:T(8,128)(2,1)S(1)}, bf16[1024,64]{0,1:T(8,128)(2,1)}, u32[]{:S(2)}) copy-start(bf16[1024,64]{0,1:T(8,128)(2,1)} %param.22) | copy-start | bytes 393220
  67.5 3.8 copy-start.2
  76.6 3.9 %copy-start.12 = (s32[2]{0:T(128)S(1)}, s32[2]{0:T(128)}, u32[]{:S(2)}) copy-start(s32[2]{0:T(128)} %param.27) | copy-start | bytes 28
  80.5 44.6 %copy-start.6 = (bf16[64,1024]{1,0:T(8,128)(2,1)S(1)}, bf16[64,1024]{1,0:T(8,128)(2,1)}, u32[]{:S(2)}) copy-start(bf16[64,1024]{1,0:T(8,128)(2,1)} %param.24) | copy-start | bytes 393220
  85.3 16.7 %copy-start.4 = (bf16[2,1024,64]{2,1,0:T(8,128)(2,1)S(1)}, bf16[2,1024,64]{2,1,0:T(8,128)(2,1)}, u32[]{:S(2)}) copy-start(bf16[2,1024,64]{2,1,0:T(8,128)(2,1)} %get-tuple-element.550) | copy-start | bytes 786436 | tf_op jit(solution)/shard_map/while
  102.0 0.8 copy-start.5
  107.5 16.7 %copy-start.4 = (bf16[2,1024,64]{2,1,0:T(8,128)(2,1)S(1)}, bf16[2,1024,64]{2,1,0:T(8,128)(2,1)}, u32[]{:S(2)}) copy-start(bf16[2,1024,64]{2,1,0:T(8,128)(2,1)} %get-tuple-element.550) | copy-start | bytes 786436 | tf_op jit(solution)/shard_map/while
  124.3 0.8 copy-start.5
  130.6 0.7 copy-start.8
  130.6 90.7 %copy-start.3 = (bf16[128,1024]{1,0:T(8,128)(2,1)S(1)}, bf16[128,1024]{1,0:T(8,128)(2,1)}, u32[]{:S(2)}) copy-start(bf16[128,1024]{1,0:T(8,128)(2,1)} %param.19) | copy-start | bytes 786436
  130.6 91.9 %copy-start.9 = (f32[1024]{0:T(1024)S(1)}, f32[1024]{0:T(1024)}, u32[]{:S(2)}) copy-start(f32[1024]{0:T(1024)} %param.21) | copy-start | bytes 12292
  130.6 164.0 %all-gather.6.cloned.1.call-start = ((), (), s32[]{:S(2)}) async-start(), calls=%async_computation.5 | async-start | bytes 4456448 | tf_op jit(solution)/shard_map/all_gather | solution.py:93
  230.5 59.3 %all-to-all-start = ((bf16[16,2,64,1024]{3,2,1,0:T(8,128)(2,1)}), bf16[16,2,64,1024]{3,2,1,0:T(8,128)(2,1)}, u32[]{:S(2)}, u32[]{:S(2)}) async-start(bf16[16,2,64,1024]{3,2,1,0:T(8,128)(2,1)} %bitcast.126), calls=%async_computation.1 | async-start | bytes 8388608 | tf_op jit(solution)/shard_map/all_to_all | solution.py:171
  235.5 70.3 %all-gather.8.cloned.1.call-start = ((), (), s32[]{:S(2)}) async-start(), calls=%async_computation.6 | async-start | bytes 2228224 | tf_op jit(solution)/shard_map/all_gather | solution.py:94
  314.7 4.7 %copy-start.10 = (f32[128,8]{0,1:T(8,128)S(1)}, f32[128,8]{0,1:T(8,128)}, u32[]{:S(2)}) copy-start(f32[128,8]{0,1:T(8,128)} %param.29) | copy-start | bytes 12292
  314.7 53.8 %all-to-all-start.1 = ((bf16[2,16,64,1024]{3,2,0,1:T(8,128)(2,1)}), bf16[2,16,64,1024]{3,2,0,1:T(8,128)(2,1)}, u32[]{:S(2)}, u32[]{:S(2)}) async-start(bf16[2,16,64,1024]{3,2,0,1:T(8,128)(2,1)} %copy.51), calls=%async_computation.2 | async-start | bytes 8388608 | tf_op jit(solution)/shard_map/all_to_all | solution.py:184
  368.5 12.0 %copy-start.1 = (bf16[1024,1024]{1,0:T(8,128)(2,1)S(1)}, bf16[1024,1024]{1,0:T(8,128)(2,1)}, u32[]{:S(2)}) copy-start(bf16[1024,1024]{1,0:T(8,128)(2,1)} %param.23) | copy-start | bytes 6291460
Sparse Core Ops, SparseCore 0:
  10.6 56.8 all-gather.3
  130.7 90.4 reduce-scatter.1
Sparse Core Ops, SparseCore 1:
  132.9 40.4 all-gather.5
  237.9 39.1 all-gather.7
where the time goes:
time: 393 us; the launch traced here: 388 us
  waiting for transfers between devices  246 us (63%)
  matrix products  47.9 us (12%)
  local copies, waits for them, and re-layouts  43 us (11%)
  other arithmetic  17.8 us (5%)
  between operations  15.1 us (4%)
  starting transfers between devices  9.99 us (3%)
  loops' own time  7.97 us (2%)
    reduce_scatter x1, waiting for transfers between devices, shards(): lax.psum_scatter(jnp.dot(attended, w_out, preferred_element_type=jnp.floa...  89.4 us
    all_to_all x1, waiting for transfers between devices, shards(): lax.all_to_all(send_buffer.reshape(tp_size, experts_local, capacity, D),...  53.7 us
    all_gather x1, waiting for transfers between devices, shards(): piece = lax.all_gather(normed, 'tp', axis=0, tiled=True)  53.4 us
    all_to_all x1, waiting for transfers between devices, shards(): lax.all_to_all(produced.reshape(experts_local, tp_size, capacity, D), 'tp...  48.9 us
    dot_general x1, matrix products, shards(): jnp.einsum('esd,edf->esf', received, gate_up_full, preferred_element_type...  11.2 us
    gather x1, local copies, waits for them, and re-layouts, shards(): picked = returned[target]  8.89 us
    scatter x1, local copies, waits for them, and re-layouts, shards(): jnp.zeros((EXPERTS * capacity, D), jnp.bfloat16).at[target]  7.92 us
    dot_general x4, matrix products, one_block(): jnp.einsum('qgpd,kgd->gpqk', block_query, keys_total, preferred_element_t...  7.91 us
  transfers between devices with their start and end apart: 6, of which 4 were waited for; matrix products, arithmetic and copies ran while one was open for 8% of the time, Pallas kernels for 0%

commit v1 on v0

v1 whole, which is shorter than its diff:
```python
import jax
import jax.numpy as jnp
from jax import lax
from jax.sharding import Mesh
from jax.sharding import PartitionSpec as P

D = 1024
HEADS = 16
KV_HEADS = 8
HEAD_DIM = 64
EXPERTS = 32
FF_EXPERT = 512
TOP = 8
NEW = 1024
MAX_CACHED = 2048
REQ_DEV = 2


ATTN_SCALE = 0.015625
EPSILON = 1e-06
THETA = 10000.0

TOK = ("tz", "tc")
TP = ("ra", "rb")


def rms_norm(values, gain):
    wide = values.astype(jnp.float32)
    factor = lax.rsqrt(jnp.mean(wide * wide, axis=-1, keepdims=True) + EPSILON)
    return (wide * factor * gain).astype(jnp.bfloat16)


def rotate(values, positions):
    row_count = values.shape[0]
    shaped = values.reshape(row_count, -1, HEAD_DIM)
    half_dim = HEAD_DIM // 2
    exponent = jnp.arange(half_dim).astype(jnp.float32) * (2.0 / HEAD_DIM)
    frequency = jnp.power(THETA, -exponent)
    angles = positions.astype(jnp.float32)[:, None] * frequency[None, :]
    cosine = jnp.cos(angles)[:, None, :]
    sine_part = jnp.sin(angles)[:, None, :]
    leading = shaped[..., :half_dim]
    trailing = shaped[..., half_dim:]
    turned = jnp.concatenate(
        [leading * cosine - trailing * sine_part, trailing * cosine + leading * sine_part], axis=-1
    )
    return turned.reshape(row_count, -1)


def shards(
    hidden_states,
    first_gain,
    second_gain,
    w_query,
    w_keyval,
    w_out,
    kv_cache,
    page_table,
    cached_len,
    expert_ids,
    gate_weights,
    w_gate_up,
    w_down,
):
    tok_rows = hidden_states.shape[0]
    tp_size = lax.axis_size(TP)
    core = lax.axis_index("tc")
    local_req = lax.axis_index("ra")
    block = lax.axis_index("rb")
    kv_cols = KV_HEADS * HEAD_DIM
    group_size = HEADS // KV_HEADS

    half_rows = D // 2
    wq_half = lax.dynamic_slice_in_dim(w_query, core * half_rows, half_rows, 0)
    wq_full = lax.all_gather(
        lax.all_gather(wq_half, TP, axis=1, tiled=True), "tc", axis=0, tiled=True
    )
    wo_half = lax.dynamic_slice_in_dim(w_out, core * half_rows, half_rows, 1)
    wo_full = lax.all_gather(
        lax.all_gather(wo_half, TP, axis=0, tiled=True), "tc", axis=1, tiled=True
    )
    gate_up_full = lax.all_gather(w_gate_up, TOK, axis=1, tiled=True)
    down_full = lax.all_gather(w_down, TOK, axis=1, tiled=True)

    normed = rms_norm(hidden_states, first_gain)
    length = cached_len[local_req]
    positions = length + block * tok_rows + jnp.arange(tok_rows, dtype=jnp.int32)
    keyval = jnp.dot(normed, w_keyval, preferred_element_type=jnp.float32)
    new_kv = jnp.concatenate(
        [rotate(keyval[:, :kv_cols], positions), keyval[:, kv_cols:]], axis=1
    ).astype(jnp.bfloat16)
    request_kv = lax.all_gather(new_kv, "rb", axis=0, tiled=True)
    queries = rotate(
        jnp.dot(normed, wq_full, preferred_element_type=jnp.float32), positions
    ).astype(jnp.bfloat16)

    local_pages = page_table[local_req] - lax.axis_index(TOK) * kv_cache.shape[0]
    cached = jnp.take(kv_cache, local_pages, axis=0).reshape(MAX_CACHED, 2 * kv_cols)
    keys_total = jnp.concatenate([cached[:, :kv_cols], request_kv[:, :kv_cols]], axis=0).reshape(
        MAX_CACHED + NEW, KV_HEADS, HEAD_DIM
    )
    values_total = jnp.concatenate(
        [cached[:, kv_cols:], request_kv[:, kv_cols:]], axis=0
    ).reshape(MAX_CACHED + NEW, KV_HEADS, HEAD_DIM)
    grouped_q = queries.reshape(tok_rows, KV_HEADS, group_size, HEAD_DIM)
    scores = (
        jnp.einsum("qgpd,kgd->gpqk", grouped_q, keys_total, preferred_element_type=jnp.float32)
        * ATTN_SCALE
    )
    key_index = jnp.arange(MAX_CACHED + NEW, dtype=jnp.int32)
    query_pos = block * tok_rows + jnp.arange(tok_rows, dtype=jnp.int32)
    allowed = jnp.where(
        key_index[None, :] < MAX_CACHED,
        key_index[None, :] < length,
        key_index[None, :] - MAX_CACHED <= query_pos[:, None],
    )
    scores = jnp.where(allowed, scores, -1e30)
    top_score = jnp.max(scores, axis=-1, keepdims=True)
    weights = jnp.exp(scores - top_score)
    probs = (weights / jnp.sum(weights, axis=-1, keepdims=True)).astype(jnp.bfloat16)
    attended = (
        jnp.einsum("gpqk,kgd->qgpd", probs, values_total, preferred_element_type=jnp.float32)
        .astype(jnp.bfloat16)
        .reshape(tok_rows, HEADS * HEAD_DIM)
    )
    projected_out = jnp.dot(attended, wo_full, preferred_element_type=jnp.float32)
    middle = (hidden_states.astype(jnp.float32) + projected_out).astype(jnp.bfloat16)
    normed_two = rms_norm(middle, second_gain)

    experts_local = EXPERTS // tp_size
    capacity = 2 * tok_rows * TOP // EXPERTS
    expert_range = jnp.arange(EXPERTS, dtype=jnp.int32)
    onehot = (expert_ids[:, :, None] == expert_range[None, None, :]).astype(jnp.int32)
    per_token = jnp.sum(onehot, axis=1)
    earlier = jnp.cumsum(per_token, axis=0) - per_token
    slot_ids = jnp.sum(onehot * earlier[:, None, :], axis=2)
    target = expert_ids * capacity + slot_ids
    outgoing_rows = jnp.broadcast_to(normed_two[:, None, :], (tok_rows, TOP, D))
    send_buffer = jnp.zeros((EXPERTS * capacity, D), jnp.bfloat16).at[target].set(outgoing_rows)
    received = lax.all_to_all(
        send_buffer.reshape(tp_size, experts_local, capacity, D),
        TP,
        split_axis=0,
        concat_axis=2,
        tiled=True,
    )
    received = received.reshape(experts_local, tp_size * capacity, D)
    both = jnp.einsum("esd,edf->esf", received, gate_up_full, preferred_element_type=jnp.float32)
    activated = (jax.nn.silu(both[..., :FF_EXPERT]) * both[..., FF_EXPERT:]).astype(jnp.bfloat16)
    produced = jnp.einsum(
        "esf,efd->esd", activated, down_full, preferred_element_type=jnp.float32
    ).astype(jnp.bfloat16)
    returned = lax.all_to_all(
        produced.reshape(experts_local, tp_size, capacity, D),
        TP,
        split_axis=1,
        concat_axis=0,
        tiled=True,
    )
    returned = returned.reshape(EXPERTS * capacity, D)
    picked = returned[target]
    mixture = jnp.einsum("tk,tkd->td", gate_weights, picked.astype(jnp.float32))
    return (middle.astype(jnp.float32) + mixture).astype(jnp.bfloat16)


def solution(mesh):
    tok_size, tp_size = mesh.devices.shape
    group = tp_size // REQ_DEV
    split = Mesh(mesh.devices.reshape(tok_size // 2, 2, REQ_DEV, group), TOK + TP)
    in_specs = (
        P(TOK + TP, None),
        P(),
        P(),
        P(None, TP),
        P(),
        P(TP, None),
        P(TOK, None, None),
        P(TOK, None),
        P(TOK),
        P(TOK + TP, None),
        P(TOK + TP, None),
        P(TP, TOK, None),
        P(TP, TOK, None),
    )
    out_specs = P(TOK + TP, None)
    return jax.shard_map(shards, mesh=split, in_specs=in_specs, out_specs=out_specs, check_vma=False)
```

time: 393 us -> 388 us (0.987)
  waiting for transfers between devices: 246 us -> 232 us
  starting transfers between devices: 9.99 us -> 21.3 us
  loops' own time: 7.97 us -> 0 us
  local copies, waits for them, and re-layouts: 43 us -> 49.4 us
    reduce_scatter x1 -> x0, waiting for transfers between devices: 89.4 us -> none  [shards(): lax.psum_scatter(jnp.dot(attended, w_out, preferred_element_type=jnp.floa...]
    all_gather x3 -> x7, waiting for transfers between devices: 53.4 us -> 121 us  [the longest x1 49.3 us: shards(): lax.all_gather(wo_half, TP, axis=0, tiled=True)]
    sub x0 -> x1, matrix products: none -> 14 us  [shards(): weights = jnp.exp(scores - top_score)]
    dot_general x12 -> x4, matrix products: 28 us -> 17.7 us  [the longest x1 11.7 us: shards(): jnp.einsum('gpqk,kgd->qgpd', probs, values_total, preferred_element_type=...]
    all_to_all x1, starting transfers between devices: 4.68 us -> 14.2 us  [shards(): lax.all_to_all(produced.reshape(experts_local, tp_size, capacity, D), TP,...]
    slice x0 -> x7, local copies, waits for them, and re-layouts: none -> 8.53 us  [the longest x2 5.25 us: shards(): request_kv[:, :kv_cols]]
    another operation x3 -> x0, loops' own time: 7.97 us -> none  [the longest x2 7.72 us: attend_request(): return lax.map(one_block, starts).reshape(NEW, -1)]
    gather x4 -> x2, local copies, waits for them, and re-layouts: 4.86 us -> 12.1 us  [shards(): jnp.take(kv_cache, local_pages, axis=0).reshape(MAX_CACHED, 2 * kv_cols)]
  transfers between devices with their start and end apart: 6 -> 9, of which waited for: 4 -> 6; matrix products, arithmetic and copies ran while one was open for 8% -> 24% of each run, Pallas kernels for 0% -> 0%
where the time goes in v1:
time: 388 us; the launch traced here: 383 us
  waiting for transfers between devices  232 us (60%)
  matrix products  51.6 us (13%)
  local copies, waits for them, and re-layouts  49.4 us (13%)
  starting transfers between devices  21.3 us (5%)
  other arithmetic  14.4 us (4%)
  between operations  14.4 us (4%)
    all_to_all x1, waiting for transfers between devices, shards(): lax.all_to_all(send_buffer.reshape(tp_size, experts_local, capacity, D),...  55.5 us
    all_to_all x1, waiting for transfers between devices, shards(): lax.all_to_all(produced.reshape(experts_local, tp_size, capacity, D), TP,...  54.2 us
    all_gather x1, waiting for transfers between devices, shards(): lax.all_gather(wo_half, TP, axis=0, tiled=True)  49.3 us
    all_gather x1, waiting for transfers between devices, shards(): lax.all_gather(wq_half, TP, axis=1, tiled=True)  42.8 us
    all_gather x1, waiting for transfers between devices, shards(): request_kv = lax.all_gather(new_kv, 'rb', axis=0, tiled=True)  22.9 us
    all_to_all x1, starting transfers between devices, shards(): lax.all_to_all(produced.reshape(experts_local, tp_size, capacity, D), TP,...  14.2 us
    sub x1, matrix products, shards(): weights = jnp.exp(scores - top_score)  14 us
    gather x2, local copies, waits for them, and re-layouts, shards(): jnp.take(kv_cache, local_pages, axis=0).reshape(MAX_CACHED, 2 * kv_cols)  12.1 us
  transfers between devices with their start and end apart: 9, of which 6 were waited for; matrix products, arithmetic and copies ran while one was open for 24% of the time, Pallas kernels for 0%

profile of v1, /device:TPU:224, one launch (start us, length us, event | category | flops | bytes accessed | tf_op | source)
XLA Modules:
  0.0 383.2 jit_solution(11292400467645476767)
XLA Ops:
  6.5 1.6 constant_dynamic-slice_fusion.1
  8.2 1.5 constant_dynamic-slice_fusion
  9.8 1.1 fusion.20
  10.9 1.4 fusion.26
  12.4 0.1 copy.44
  12.5 0.6 dynamic_slice.13
  13.8 0.1 multiply_cosine_fusion
  14.0 0.1 copy.45
  14.1 0.7 pad_maximum_fusion.2
  14.9 42.8 %all-gather.10.cloned.1.call-done = bf16[512,1024]{0,1:T(8,128)(2,1)} async-done(((bf16[512,64]{0,1:T(8,128)(2,1)}), bf16[512,1024]{0,1:T(8,128)(2,1)}) %all-gather.10.cloned.1.call-update) | async-done | bytes 1048592 | tf_op jit(solution)/shard_map/all_gather | solution.py:76
  57.8 49.3 %all-gather.14.cloned.1.call-done = bf16[1024,512]{1,0:T(8,128)(2,1)} async-done(((bf16[64,512]{1,0:T(8,128)(2,1)}), bf16[1024,512]{1,0:T(8,128)(2,1)}) %all-gather.14.cloned.1.call-update) | async-done | bytes 1048592 | tf_op jit(solution)/shard_map/all_gather | solution.py:80
  107.1 0.5 all-gather.18.cloned.1.call-update
  107.7 0.6 iota_compare_fusion.1
  108.4 5.5 %gather_fusion = bf16[16,128,1024]{2,1,0:T(8,128)(2,1)} fusion(bf16[24,128,1024]{2,1,0:T(8,128)(2,1)} %param.19, s32[1024]{0:T(1024)S(1)} %pad_clamp_fusion), kind=kCustom, calls=%fused_computation | custom fusion | bytes 8388672 | tf_op jit(solution)/shard_map/jit(_take)/gather | solution.py:98
  113.9 6.6 %copy.43 = bf16[2048,1024]{0,1:T(8,128)(2,1)} copy(bf16[2048,1024]{1,0:T(8,128)(2,1)} %bitcast.74) | data formatting | bytes 8388608 | tf_op jit(solution)/shard_map/jit(_take)/gather | solution.py:98
  120.6 2.6 broadcast_select_fusion
  123.2 1.6 fusion.33
  124.8 0.1 copy.50
  124.9 0.2 reduce_window_sum.11
  125.2 3.5 compare_select_fusion
  128.8 0.1 copy.53
  128.9 0.1 reshape.206
  129.0 22.9 %all-gather.8.cloned.1.call-done = bf16[1024,1024]{1,0:T(8,128)(2,1)} async-done(((bf16[128,1024]{1,0:T(8,128)(2,1)}), bf16[1024,1024]{1,0:T(8,128)(2,1)}) %all-gather.8.cloned.1.call-update) | async-done | bytes 2097168 | tf_op jit(solution)/shard_map/all_gather | solution.py:92
  151.8 3.0 fusion.34
  154.8 1.5 copy.46
  156.3 2.3 copy.47
  158.6 4.3 %pad_maximum_fusion = (bf16[3072,512]{0,1:T(8,128)(2,1)}, bf16[3072,512]{0,1:T(8,128)(2,1)}) fusion(bf16[1024,512]{0,1:T(8,128)(2,1)S(1)} %copy.46, bf16[2048,512]{0,1:T(8,128)(2,1)} %get-tuple-element.6, bf16[1024,512]{0,1:T(8,128)(2,1)} %copy.47, bf16[2048,512]{0,1:T(8,128)(2,1)S(1)} %get-tuple-element.5), kind=kLoop, calls=%fused_computation.15 | loop fusion | flops 12582912 | bytes 12582912 | tf_op jit(solution)/shard_map/concatenate | solution.py:102
  162.9 6.2 %all-gather.12.cloned.1.call-done = bf16[1024,1024]{0,1:T(8,128)(2,1)} async-done(((bf16[512,1024]{0,1:T(8,128)(2,1)}), bf16[1024,1024]{0,1:T(8,128)(2,1)}) %all-gather.12.cloned.1.call-update) | async-done | bytes 2097168 | tf_op jit(solution)/shard_map/all_gather | solution.py:75
  169.1 2.4 fusion.24
  171.5 0.1 subtract_convert_fusion
  171.6 14.0 %fusion.35 = (f32[8,2,128]{2,1,0:T(2,128)S(1)}, f32[8,2,128,3072]{2,3,1,0:T(8,128)}) fusion(pred[128,3072]{0,1:T(8,128)(4,1)S(1)} %copy-done.3, bf16[3072,8,64,1]{0,2,3,1:T(8,128)(2,1)} %bitcast.78, bf16[128,8,2,64]{0,3,2,1:T(8,128)(2,1)S(1)} %bitcast.82), kind=kOutput, calls=%fused_computation.80 | convolution fusion | flops 830475264 | bytes 28975104 | tf_op jit(solution)/shard_map/sub | solution.py:119
  185.6 11.7 %fusion.18 = bf16[8,64,2,128]{3,1,2,0:T(8,128)(2,1)S(1)} fusion(bf16[3072,8,64,1]{0,2,3,1:T(8,128)(2,1)} %bitcast.77, f32[8,2,128,3072]{2,3,1,0:T(8,128)} %get-tuple-element.16, f32[8,2,128]{2,1,0:T(2,128)S(1)} %get-tuple-element.15), kind=kOutput, calls=%fused_computation.29 | convolution fusion | flops 818020352 | bytes 28581888 | tf_op jit(solution)/shard_map/gpqk,kgd->qgpd/dot_general | solution.py:122
  197.3 2.1 multiply_reduce_fusion
  199.5 0.1 multiply_convert_fusion
  199.6 8.1 %scatter_custom_fusion = bf16[2048,1024]{1,0:T(8,128)(2,1)} fusion(s32[1024]{0:T(1024)S(1)} %reshape.206, bf16[]{:T(256)} %constant.75.clone.1, bf16[128,1024]{1,0:T(8,128)(2,1)S(1)} %multiply_convert_fusion), kind=kCustom, calls=%fused_computation.21 | custom fusion | bytes 4456450 | tf_op jit(solution)/shard_map/scatter | solution.py:139
  207.7 6.9 %all-to-all-start = ((bf16[16,2,64,1024]{3,2,1,0:T(8,128)(2,1)}), bf16[16,2,64,1024]{3,2,1,0:T(8,128)(2,1)}, u32[]{:S(2)}, u32[]{:S(2)}) async-start(bf16[16,2,64,1024]{3,2,1,0:T(8,128)(2,1)} %bitcast.73), calls=%async_computation | async-start | bytes 8388608 | tf_op jit(solution)/shard_map/all_to_all | solution.py:140
  214.7 0.7 all-gather.20.cloned.1.call-update
  215.4 55.5 %all-to-all-done = bf16[16,2,64,1024]{3,2,1,0:T(8,128)(2,1)} async-done(((bf16[16,2,64,1024]{3,2,1,0:T(8,128)(2,1)}), bf16[16,2,64,1024]{3,2,1,0:T(8,128)(2,1)}, u32[]{:S(2)}, u32[]{:S(2)}) %all-to-all-start) | async-done | bytes 4194336 | tf_op jit(solution)/shard_map/all_to_all | solution.py:140
  270.9 4.9 %copy.54 = bf16[1,2,16,64,1024]{4,3,2,1,0:T(8,128)(2,1)} copy(bf16[1,2,16,64,1024]{4,3,1,2,0:T(8,128)(2,1)} %bitcast.22) | data formatting | bytes 8388608 | tf_op jit(solution)/shard_map/all_to_all | solution.py:140
  275.7 11.2 %fusion.36 = f32[2,1024,1024]{2,1,0:T(8,128)} fusion(bf16[2,1024,1024]{2,1,0:T(8,128)(2,1)} %bitcast.75, bf16[2,1024,1024]{2,1,0:T(8,128)(2,1)} %all-gather.18.cloned.1.call-done), kind=kOutput, calls=%fused_computation.81 | convolution fusion | flops 4294967296 | bytes 16777216 | tf_op jit(solution)/shard_map/esd,edf->esf/dot_general | solution.py:148
  286.9 6.4 %convolution_convert_fusion = bf16[2,1024,1024]{2,1,0:T(8,128)(2,1)S(1)} fusion(bf16[2,512,1024]{2,1,0:T(8,128)(2,1)} %all-gather.20.cloned.1.call-done, f32[2,1024,1024]{2,1,0:T(8,128)} %fusion.36), kind=kOutput, calls=%fused_computation.18 | convolution fusion | flops 2155872256 | bytes 14680064 | tf_op jit(solution)/shard_map/esf,efd->esd/dot_general | solution.py:150
  293.4 2.5 copy.55
  295.8 14.2 %all-to-all-start.1 = ((bf16[2,16,64,1024]{3,2,0,1:T(8,128)(2,1)}), bf16[2,16,64,1024]{3,2,0,1:T(8,128)(2,1)}, u32[]{:S(2)}, u32[]{:S(2)}) async-start(bf16[2,16,64,1024]{3,2,0,1:T(8,128)(2,1)} %copy.55), calls=%async_computation.1 | async-start | bytes 8388608 | tf_op jit(solution)/shard_map/all_to_all | solution.py:153
  310.0 0.1 copy.60
  310.2 54.2 %all-to-all-done.1 = bf16[2,16,64,1024]{3,2,0,1:T(8,128)(2,1)} async-done(((bf16[2,16,64,1024]{3,2,0,1:T(8,128)(2,1)}), bf16[2,16,64,1024]{3,2,0,1:T(8,128)(2,1)}, u32[]{:S(2)}, u32[]{:S(2)}) %all-to-all-start.1) | async-done | bytes 4194336 | tf_op jit(solution)/shard_map/all_to_all | solution.py:153
  364.4 8.9 %gather_fusion.1 = bf16[1024,1024]{1,0:T(8,128)(2,1)} fusion(bf16[2048,1024]{1,0:T(8,128)(2,1)} %bitcast.27, s32[1024]{0:T(1024)S(1)} %broadcast_clamp_fusion), kind=kCustom, calls=%fused_computation.1 | custom fusion | bytes 4198400 | tf_op jit(solution)/shard_map/gather | solution.py:161
  373.3 2.3 fusion.10
  375.6 0.8 fusion.23
  (56 shorter events, 0.8 us)
Async XLA Ops:
  6.5 4.3 %copy-start = (bf16[1024,1024]{1,0:T(8,128)(2,1)S(1)}, bf16[1024,1024]{1,0:T(8,128)(2,1)}, u32[]{:S(2)}) copy-start(bf16[1024,1024]{1,0:T(8,128)(2,1)} %param.17) | copy-start | bytes 6291460
  6.5 6.0 %copy-start.9 = (s32[2]{0:T(128)S(1)}, s32[2]{0:T(128)}, u32[]{:S(2)}) copy-start(s32[2]{0:T(128)} %param.21) | copy-start | bytes 28
  6.5 51.2 %all-gather.10.cloned.1.call-start = ((), (), s32[]{:S(2)}) async-start(), calls=%async_computation.3 | async-start | bytes 1114112 | tf_op jit(solution)/shard_map/all_gather | solution.py:76
  8.2 98.9 %all-gather.14.cloned.1.call-start = ((), (), s32[]{:S(2)}) async-start(), calls=%async_computation.5 | async-start | bytes 1114112 | tf_op jit(solution)/shard_map/all_gather | solution.py:80
  9.7 142.1 %all-gather.8.cloned.1.call-start = ((), (), s32[]{:S(2)}) async-start(), calls=%async_computation.2 | async-start | bytes 2359296 | tf_op jit(solution)/shard_map/all_gather | solution.py:92
  10.9 96.8 %copy-start.8 = (s32[2,16]{1,0:T(2,128)S(1)}, s32[2,16]{1,0:T(2,128)}, u32[]{:S(2)}) copy-start(s32[2,16]{1,0:T(2,128)} %param.20) | copy-start | bytes 388
  14.9 154.2 %all-gather.12.cloned.1.call-start = ((), (), s32[]{:S(2)}) async-start(), calls=%async_computation.4 | async-start | bytes 3145728 | tf_op jit(solution)/shard_map/all_gather | solution.py:75
  57.7 139.6 %all-gather.16.cloned.1.call-start = ((), (), s32[]{:S(2)}) async-start(), calls=%async_computation.6 | async-start | bytes 3145728 | tf_op jit(solution)/shard_map/all_gather | solution.py:79
  107.1 168.6 %all-gather.18.cloned.1.call-start = ((), (), s32[]{:S(2)}) async-start(), calls=%async_computation.7 | async-start | bytes 4456448 | tf_op jit(solution)/shard_map/all_gather | solution.py:82
  123.2 1.7 copy-start.4
  158.6 10.5 %copy-start.2 = (bf16[128,1024]{1,0:T(8,128)(2,1)S(1)}, bf16[128,1024]{1,0:T(8,128)(2,1)}, u32[]{:S(2)}) copy-start(bf16[128,1024]{1,0:T(8,128)(2,1)} %param.13) | copy-start | bytes 786436
  158.6 10.5 %copy-start.5 = (f32[1024]{0:T(1024)S(1)}, f32[1024]{0:T(1024)}, u32[]{:S(2)}) copy-start(f32[1024]{0:T(1024)} %param.14) | copy-start | bytes 12292
  162.9 8.7 %copy-start.3 = (pred[128,3072]{0,1:T(8,128)(4,1)S(1)}, pred[128,3072]{0,1:T(8,128)(4,1)}, u32[]{:S(2)}) copy-start(pred[128,3072]{0,1:T(8,128)(4,1)} %compare_select_fusion) | copy-start | bytes 1179652
  185.6 13.9 %copy-start.6 = (f32[1024]{0:T(1024)S(1)}, f32[1024]{0:T(1024)}, u32[]{:S(2)}) copy-start(f32[1024]{0:T(1024)} %param.15) | copy-start | bytes 12292
  207.7 63.1 %all-to-all-start = ((bf16[16,2,64,1024]{3,2,1,0:T(8,128)(2,1)}), bf16[16,2,64,1024]{3,2,1,0:T(8,128)(2,1)}, u32[]{:S(2)}, u32[]{:S(2)}) async-start(bf16[16,2,64,1024]{3,2,1,0:T(8,128)(2,1)} %bitcast.73), calls=%async_computation | async-start | bytes 8388608 | tf_op jit(solution)/shard_map/all_to_all | solution.py:140
  214.6 72.3 %all-gather.20.cloned.1.call-start = ((), (), s32[]{:S(2)}) async-start(), calls=%async_computation.8 | async-start | bytes 2228224 | tf_op jit(solution)/shard_map/all_gather | solution.py:83
  295.8 14.2 %copy-start.7 = (f32[128,8]{0,1:T(8,128)S(1)}, f32[128,8]{0,1:T(8,128)}, u32[]{:S(2)}) copy-start(f32[128,8]{0,1:T(8,128)} %param.23) | copy-start | bytes 12292
  295.8 68.5 %all-to-all-start.1 = ((bf16[2,16,64,1024]{3,2,0,1:T(8,128)(2,1)}), bf16[2,16,64,1024]{3,2,0,1:T(8,128)(2,1)}, u32[]{:S(2)}, u32[]{:S(2)}) async-start(bf16[2,16,64,1024]{3,2,0,1:T(8,128)(2,1)} %copy.55), calls=%async_computation.1 | async-start | bytes 8388608 | tf_op jit(solution)/shard_map/all_to_all | solution.py:153
  364.4 12.0 %copy-start.1 = (bf16[1024,1024]{1,0:T(8,128)(2,1)S(1)}, bf16[1024,1024]{1,0:T(8,128)(2,1)}, u32[]{:S(2)}) copy-start(bf16[1024,1024]{1,0:T(8,128)(2,1)} %param.17) | copy-start | bytes 6291460
Sparse Core Ops, SparseCore 0:
  9.8 47.8 all-gather.9
  60.1 46.8 all-gather.13
  108.8 42.9 all-gather.7
  153.5 15.5 all-gather.11
  170.7 17.1 all-gather.15
  189.7 41.9 all-gather.17
  233.5 37.4 all-gather.19
